TPU v7x, 256 devices: a whole 4x4x8 slice. The times are simulated.
256 devices in a mesh: pair: 32 (over y, x, core), lam: 8 (over z).
Axes of the slice: x: 4, y: 4, z: 8, core: 2. Of those that a mesh axis runs over, the one named last changes fastest.
Arguments:
- integrals: bfloat16 [32, 64, 4, 64, 1024], P('pair', 'lam'), may hold values from -0.119628906 to 0.119628906
- tile_pair: int32 [32, 64], P('pair', 'lam'), may hold values from 0 to 15, as said below
- tile_lam: int32 [32, 64], P('pair', 'lam'), may hold values from 0 to 15, as said below
- tile_count: int32 [32, 8], P('pair', 'lam'), may hold values from 1 to 8, as said below
- mu_index: int32 [2048], P('pair'), may hold values from 0 to 1023
- nu_index: int32 [2048], P('pair'), may hold values from 0 to 1023
- occupied_coef: bfloat16 [1024, 16], replicated, may hold values from -1.5 to 1.5
- virtual_coef: bfloat16 [1024, 1280], replicated, may hold values from -1.5 to 1.5
Outputs:
- orbital_integrals: float32 [16, 1280, 20480], P('lam', 'pair')
Inputs may be any that keep to these rules, and one draw needn't show every extreme that they name: On every device the live and dead slots name distinct pairs of (tile_pair, tile_lam); tile_pair lies in 0 to 15. On lam index l every slot's tile_lam lies in l * 2 to (l + 1) * 2 - 1. Slots from tile_count on are dead and their integrals are ignored; some device has all 8 slots live.
All inputs are finite; a program needn't handle non-finite values.
Results may differ from a plain program's by a relative error of at most 0.0049.
Values may be sent and summed in bfloat16 or wider, within the bound.
No kernel may reach another device: no remote copies, remote signals or barrier semaphores. Data moves between devices by JAX's collectives and lax.ppermute only.
A program may use at most 128 MiB of HBM per device.

v0:
```python
import jax
import jax.numpy as jnp
from jax import lax
from jax.sharding import PartitionSpec as P


def on_device(
    integrals, tile_pair, tile_lam, tile_count, mu_index, nu_index, occupied_coef, virtual_coef
):
    lam_count = lax.axis_size("lam")
    pair_count = lax.axis_size("pair")
    basis_count, occ_total = occupied_coef.shape
    vir_total = virtual_coef.shape[1]
    rows_here = mu_index.shape[0]
    occ_share = occ_total // lam_count
    vir_share = vir_total // pair_count
    tile_data = integrals[0]
    slot_count, tile_rows, tile_depth, _ = tile_data.shape
    block_count = rows_here // tile_rows
    pair_list = tile_pair[0]
    lam_list = tile_lam[0]
    live = jnp.arange(slot_count) < tile_count[0, 0]
    occ_blocks = occupied_coef.reshape(basis_count // tile_depth, tile_depth, occ_total)
    occ_slot = jnp.take(occ_blocks, lam_list, axis=0)
    occ_slot = jnp.where(live[:, None, None], occ_slot, jnp.zeros((), occ_slot.dtype))
    contrib = jnp.einsum("tmj,tkms->jtks", occ_slot, tile_data, preferred_element_type=jnp.float32)
    peak = jnp.maximum(jnp.max(jnp.abs(contrib)), 1e-30)
    exponent = jnp.clip(jnp.floor(jnp.log2(peak)), -100.0, 100.0)
    scale = jnp.exp2(13.0 - exponent)
    payload = (
        (contrib * scale)
        .astype(jnp.float16)
        .reshape(lam_count, occ_share, slot_count, tile_rows, basis_count)
    )
    hit = (pair_list[:, None] == jnp.arange(block_count)[None, :]) & live[:, None]
    info = jnp.zeros((slot_count, 128), jnp.float32)
    info = info.at[:, :block_count].set(hit.astype(jnp.float32))
    info = info.at[:, block_count].set(exponent)
    info = jnp.broadcast_to(
        info.astype(jnp.float16)[None, None, :, None, :],
        (lam_count, occ_share, slot_count, tile_rows, 128),
    )
    payload = jnp.concatenate([payload, info], axis=4)
    own_rows = jnp.zeros((2, pair_count, rows_here), jnp.float32)
    own_rows = lax.dynamic_update_index_in_dim(
        own_rows,
        jnp.stack([mu_index, nu_index]).astype(jnp.float32)[:, None],
        lax.axis_index("pair"),
        1,
    )
    both_index = lax.psum(own_rows, "pair").astype(jnp.int32).reshape(2, pair_count * rows_here)
    got = lax.all_to_all(payload, "lam", split_axis=0, concat_axis=0, tiled=True)
    got_info = got[:, 0, :, 0, basis_count:].astype(jnp.float32)
    unscale = jnp.exp2(got_info[:, 0, block_count] - 13.0)
    got_hit = got_info[:, :, :block_count] * unscale[:, None, None]
    own_half = jnp.einsum(
        "ptg,pjtks->jgks",
        got_hit,
        got[..., :basis_count].astype(jnp.float32),
        precision=lax.Precision.HIGHEST,
        preferred_element_type=jnp.float32,
    ).reshape(occ_share, rows_here, basis_count)
    half_low = own_half.astype(jnp.bfloat16).reshape(occ_share * rows_here, basis_count)
    mixed = jnp.dot(half_low, virtual_coef, preferred_element_type=jnp.float32)
    mixed = mixed.astype(jnp.bfloat16).reshape(occ_share, rows_here, pair_count, vir_share)
    received = lax.all_to_all(mixed, "pair", split_axis=2, concat_axis=1, tiled=True)
    total_rows = received.shape[1]
    mixed_rows = received.reshape(occ_share, total_rows, vir_share)
    occ_rows = jnp.take(occupied_coef, both_index[0], axis=0)
    vir_rows = jnp.take(virtual_coef, both_index[1], axis=0)
    scaled = (
        mixed_rows.astype(jnp.float32)[:, :, :, None]
        * occ_rows.astype(jnp.float32)[None, :, None, :]
    ).astype(jnp.bfloat16)
    result = jnp.einsum("qrbi,ra->qbia", scaled, vir_rows, preferred_element_type=jnp.float32)
    return result.reshape(occ_share, vir_share, occ_total * vir_total)


def solution(mesh):
    placed = (
        P("pair", "lam", None, None, None),
        P("pair", "lam"),
        P("pair", "lam"),
        P("pair", "lam"),
        P("pair"),
        P("pair"),
        P(),
        P(),
    )
    return jax.shard_map(
        on_device, mesh=mesh, in_specs=placed, out_specs=P("lam", "pair", None), check_vma=False
    )
```

profile of v0, /device:TPU:1, one launch (start us, length us, event | category | flops | bytes accessed | tf_op | source)
XLA Modules:
  0.0 209.2 jit_solution(5575800816990912734)
XLA Ops:
  0.0 0.7 compare_reduce_fusion.1
  2.0 0.7 fusion.28
  2.7 0.7 compare_and_fusion.2
  3.3 0.9 reshape.236
  4.8 4.9 %abs_reduce_fusion = (f32[]{:T(128)}, f32[8,16,4,1024]{3,1,2,0:T(8,128)}) fusion(bf16[1,8,4,64,1024]{4,3,2,1,0:T(8,128)(2,1)} %param.12, bf16[8,64,16]{1,2,0:T(8,128)(2,1)S(1)} %gather_fusion, pred[8]{0:T(512)(128)(4,1)S(1)} %get-tuple-element.33, pred[8]{0:T(512)(128)(4,1)S(1)} %get-tuple-element.34), kind=kOutput, calls=%fused_computation.15 | convolution fusion | flops 68173824 | bytes 6307860 | tf_op jit(solution)/shard_map/tmj,tkms->jtks/dot_general | solution.py:26
  10.4 0.8 convert_select_fusion
  11.8 1.9 fusion.11
  13.6 1.6 copy.45
  15.4 2.6 %pad_maximum_fusion = f16[8,2,8,4,1152]{4,2,3,1,0:T(8,128)(2,1)} fusion(f16[8,2,8,4,128]{4,2,3,1,0:T(8,128)(2,1)S(1)} %broadcast_in_dim.64, f16[8,2,8,4,1024]{4,2,3,1,0:T(8,128)(2,1)} %bitcast.76), kind=kLoop, calls=%fused_computation.19 | loop fusion | flops 589824 | bytes 2359296 | tf_op jit(solution)/shard_map/concatenate | solution.py:43
  17.9 9.0 %all-to-all-start = ((f16[8,2,8,4,1152]{4,2,3,1,0:T(8,128)(2,1)}), f16[8,2,8,4,1152]{4,2,3,1,0:T(8,128)(2,1)}, u32[]{:S(2)}, u32[]{:S(2)}) async-start(f16[8,2,8,4,1152]{4,2,3,1,0:T(8,128)(2,1)} %pad_maximum_fusion), calls=%async_computation | async-start | bytes 2359296 | tf_op jit(solution)/shard_map/all_to_all | solution.py:52
  27.0 123.8 %psum.7 = f32[2,32,64]{2,1,0:T(8,128)S(1)} all-reduce(f32[2,32,64]{2,1,0:T(8,128)S(1)} %dynamic_update_slice.4), channel_id=1, replica_groups=mesh['pair'=32,'lam'=8] {'pair'}, use_global_device_ids=true, to_apply=%region_3.4 | all-reduce | flops 4096 | bytes 32768 | tf_op jit(solution)/shard_map/psum | solution.py:51
  151.3 6.2 %gather_fusion.1 = bf16[2048,16]{1,0:T(8,128)(2,1)S(1)} fusion(bf16[1024,16]{1,0:T(8,128)(2,1)S(1)} %copy.39, s32[2048]{0:T(1024)S(1)} %broadcast_clamp_fusion.1), kind=kCustom, calls=%fused_computation.1 | custom fusion | bytes 139264 | tf_op jit(solution)/shard_map/jit(_take)/gather | solution.py:69
  157.8 0.7 fusion.20
  158.7 2.2 %fusion.10 = bf16[2,16,4,1024]{3,1,2,0:T(8,128)(2,1)S(1)} fusion(f16[8,2,8,4,1152]{4,2,3,1,0:T(8,128)(2,1)} %all-to-all-done, f32[8,8,128]{2,1,0:T(8,128)S(1)} %fusion.20, f32[8]{0:T(128)S(1)} %fusion.26), kind=kOutput, calls=%fused_computation.20 | convolution fusion | flops 100795392 | bytes 1343520 | tf_op jit(solution)/shard_map/ptg,pjtks->jgks/dot_general | solution.py:56
  161.7 0.9 copy.37
  162.6 1.3 reshape.238
  163.9 1.1 reshape.272
  165.0 9.8 %all-to-all-start.1 = ((bf16[32,2,2560]{2,1,0:T(2,128)(2,1)}), bf16[32,2,2560]{2,1,0:T(2,128)(2,1)}, u32[]{:S(2)}, u32[]{:S(2)}) async-start(bf16[32,2,2560]{2,1,0:T(2,128)(2,1)} %reshape.272), calls=%async_computation.1 | async-start | bytes 655360 | tf_op jit(solution)/shard_map/all_to_all | solution.py:66
  174.9 9.8 %gather_fusion.2 = bf16[2048,1280]{1,0:T(8,128)(2,1)} fusion(bf16[1024,1280]{1,0:T(8,128)(2,1)S(1)} %copy-done, s32[2048]{0:T(1024)S(1)} %broadcast_clamp_fusion), kind=kCustom, calls=%fused_computation.2 | custom fusion | bytes 10493952 | tf_op jit(solution)/shard_map/jit(_take)/gather | solution.py:70
  184.8 1.4 reshape.273
  186.7 1.5 copy.38
  188.2 1.7 reshape.241
  189.9 11.6 %fusion = f32[2,40,16,1280]{3,2,1,0:T(8,128)} fusion(bf16[2048,1280]{1,0:T(8,128)(2,1)} %gather_fusion.2, f32[2048,16]{0,1:T(8,128)S(1)} %select_convert_fusion, f32[2,2048,40]{1,2,0:T(8,128)S(1)} %reshape.241, pred[2048]{0:T(1024)(128)(4,1)S(1)} %compare_and_fusion), kind=kOutput, calls=%fused_computation.4 | convolution fusion | flops 6718750720 | bytes 12584960 | tf_op jit(solution)/shard_map/qrbi,ra->qbia/dot_general | solution.py:75
  201.5 7.7 %reshape.239 = f32[2,40,20480]{2,1,0:T(8,128)} reshape(f32[2,40,16,1280]{3,2,1,0:T(8,128)} %fusion) | data formatting | bytes 13107200 | tf_op jit(solution)/shard_map/reshape | solution.py:76
  (44 shorter events, 3.6 us)
Async XLA Ops:
  0.0 161.2 %copy-start = (bf16[1024,1280]{1,0:T(8,128)(2,1)S(1)}, bf16[1024,1280]{1,0:T(8,128)(2,1)}, u32[]{:S(2)}) copy-start(bf16[1024,1280]{1,0:T(8,128)(2,1)} %param.19) | copy-start | bytes 7864324
  4.8 5.6 %copy-start.4 = (s32[1,8]{1,0:T(1,128)S(1)}, s32[1,8]{1,0:T(1,128)}, u32[]{:S(2)}) copy-start(s32[1,8]{1,0:T(1,128)} %param.13) | copy-start | bytes 100
  15.2 11.7 %copy-start.2 = (s32[64]{0:T(128)S(1)}, s32[64]{0:T(128)}, u32[]{:S(2)}) copy-start(s32[64]{0:T(128)} %param.17) | copy-start | bytes 772
  15.2 11.7 %copy-start.3 = (s32[64]{0:T(128)S(1)}, s32[64]{0:T(128)}, u32[]{:S(2)}) copy-start(s32[64]{0:T(128)} %param.16) | copy-start | bytes 772
  15.2 135.8 %copy-start.1 = (bf16[1024,16]{0,1:T(8,128)(2,1)S(1)}, bf16[1024,16]{0,1:T(8,128)(2,1)}, u32[]{:S(2)}) copy-start(bf16[1024,16]{0,1:T(8,128)(2,1)} %param.18) | copy-start | bytes 98308
  17.9 139.8 %all-to-all-start = ((f16[8,2,8,4,1152]{4,2,3,1,0:T(8,128)(2,1)}), f16[8,2,8,4,1152]{4,2,3,1,0:T(8,128)(2,1)}, u32[]{:S(2)}, u32[]{:S(2)}) async-start(f16[8,2,8,4,1152]{4,2,3,1,0:T(8,128)(2,1)} %pad_maximum_fusion), calls=%async_computation | async-start | bytes 2359296 | tf_op jit(solution)/shard_map/all_to_all | solution.py:52
  165.0 19.8 %all-to-all-start.1 = ((bf16[32,2,2560]{2,1,0:T(2,128)(2,1)}), bf16[32,2,2560]{2,1,0:T(2,128)(2,1)}, u32[]{:S(2)}, u32[]{:S(2)}) async-start(bf16[32,2,2560]{2,1,0:T(2,128)(2,1)} %reshape.272), calls=%async_computation.1 | async-start | bytes 655360 | tf_op jit(solution)/shard_map/all_to_all | solution.py:66
where the time goes:
time: 210 us; the launch traced here: 209 us
  blocking collectives  124 us (59%)
  local copies, waits for them, and re-layouts  35.8 us (17%)
  matrix products  19.2 us (9%)
  starting transfers between devices  18.8 us (9%)
  other arithmetic  9.33 us (4%)
  between operations  2.18 us (1%)
    psum x1, blocking collectives, on_device(): lax.psum(own_rows, 'pair').astype(jnp.int32)  124 us
    dot_general x1, matrix products, on_device(): jnp.einsum('qrbi,ra->qbia', scaled, vir_rows, preferred_element_type=jnp....  11.6 us
    gather x1, local copies, waits for them, and re-layouts, on_device(): vir_rows = jnp.take(virtual_coef, both_index[1], axis=0)  9.85 us
    all_to_all x1, starting transfers between devices, on_device(): lax.all_to_all(mixed, 'pair', split_axis=2, concat_axis=1, tiled=True)  9.83 us
    all_to_all x1, starting transfers between devices, on_device(): lax.all_to_all(payload, 'lam', split_axis=0, concat_axis=0, tiled=True)  9.01 us
    reshape x1, local copies, waits for them, and re-layouts, on_device(): return result.reshape(occ_share, vir_share, occ_total * vir_total)  7.69 us
    gather x2, local copies, waits for them, and re-layouts, on_device(): occ_rows = jnp.take(occupied_coef, both_index[0], axis=0)  6.36 us
    dot_general x1, matrix products, on_device(): jnp.einsum('tmj,tkms->jtks', occ_slot, tile_data, preferred_element_type=...  4.87 us
  transfers between devices with their start and end apart: 2, of which 0 were waited for; matrix products, arithmetic and copies ran while one was open for 8% of the time, Pallas kernels for 0%

commit v1 on v0

--- a/solution.py
+++ b/solution.py
@@ -2,6 +2,11 @@
 import jax.numpy as jnp
 from jax import lax
 from jax.sharding import PartitionSpec as P
+
+
+def gather_and_add(array, name):
+    shards = lax.all_gather(array, name)
+    return jnp.sum(shards, axis=0)
 
 
 def on_device(
@@ -48,7 +53,9 @@
         lax.axis_index("pair"),
         1,
     )
-    both_index = lax.psum(own_rows, "pair").astype(jnp.int32).reshape(2, pair_count * rows_here)
+    both_index = (
+        gather_and_add(own_rows, "pair").astype(jnp.int32).reshape(2, pair_count * rows_here)
+    )
     got = lax.all_to_all(payload, "lam", split_axis=0, concat_axis=0, tiled=True)
     got_info = got[:, 0, :, 0, basis_count:].astype(jnp.float32)
     unscale = jnp.exp2(got_info[:, 0, block_count] - 13.0)

time: 210 us -> 111 us (0.53)
  blocking collectives: 124 us -> 28.3 us
  starting transfers between devices: 18.8 us -> 14.2 us
    psum x1 -> x0, blocking collectives: 124 us -> none  [on_device(): lax.psum(own_rows, 'pair').astype(jnp.int32)]
    all_gather x0 -> x1, blocking collectives: none -> 28.3 us  [gather_and_add(): shards = lax.all_gather(array, name)]
    all_to_all x1, starting transfers between devices: 9.83 us -> 5.21 us  [on_device(): lax.all_to_all(mixed, 'pair', split_axis=2, concat_axis=1, tiled=True)]
  transfers between devices with their start and end apart: 2 -> 2, of which waited for: 0 -> 0; matrix products, arithmetic and copies ran while one was open for 8% -> 16% of each run, Pallas kernels for 0% -> 0%
where the time goes in v1:
time: 111 us; the launch traced here: 110 us
  local copies, waits for them, and re-layouts  35.8 us (32%)
  blocking collectives  28.3 us (25%)
  matrix products  19.2 us (17%)
  starting transfers between devices  14.2 us (13%)
  other arithmetic  10.7 us (10%)
  between operations  2.19 us (2%)
    all_gather x1, blocking collectives, gather_and_add(): shards = lax.all_gather(array, name)  28.3 us
    dot_general x1, matrix products, on_device(): jnp.einsum('qrbi,ra->qbia', scaled, vir_rows, preferred_element_type=jnp....  11.6 us
    gather x1, local copies, waits for them, and re-layouts, on_device(): vir_rows = jnp.take(virtual_coef, both_index[1], axis=0)  9.85 us
    all_to_all x1, starting transfers between devices, on_device(): lax.all_to_all(payload, 'lam', split_axis=0, concat_axis=0, tiled=True)  9.01 us
    reshape x1, local copies, waits for them, and re-layouts, on_device(): return result.reshape(occ_share, vir_share, occ_total * vir_total)  7.69 us
    gather x2, local copies, waits for them, and re-layouts, on_device(): occ_rows = jnp.take(occupied_coef, both_index[0], axis=0)  6.36 us
    all_to_all x1, starting transfers between devices, on_device(): lax.all_to_all(mixed, 'pair', split_axis=2, concat_axis=1, tiled=True)  5.21 us
    dot_general x1, matrix products, on_device(): jnp.einsum('tmj,tkms->jtks', occ_slot, tile_data, preferred_element_type=...  4.87 us
  transfers between devices with their start and end apart: 2, of which 0 were waited for; matrix products, arithmetic and copies ran while one was open for 16% of the time, Pallas kernels for 0%

profile of v1, /device:TPU:1, one launch (start us, length us, event | category | flops | bytes accessed | tf_op | source)
XLA Modules:
  0.0 110.3 jit_solution(9049036390914535623)
XLA Ops:
  0.0 0.7 compare_reduce_fusion.1
  2.7 0.7 compare_and_fusion.2
  3.3 0.9 reshape.242
  4.8 4.9 %abs_reduce_fusion = (f32[]{:T(128)}, f32[8,16,4,1024]{3,1,2,0:T(8,128)}) fusion(bf16[1,8,4,64,1024]{4,3,2,1,0:T(8,128)(2,1)} %param.12, bf16[8,64,16]{1,2,0:T(8,128)(2,1)S(1)} %gather_fusion, pred[8]{0:T(512)(128)(4,1)S(1)} %get-tuple-element.33, pred[8]{0:T(512)(128)(4,1)S(1)} %get-tuple-element.34), kind=kOutput, calls=%fused_computation.15 | convolution fusion | flops 68173824 | bytes 6307860 | tf_op jit(solution)/shard_map/tmj,tkms->jtks/dot_general | solution.py:31
  10.4 0.8 convert_select_fusion
  11.8 1.9 %fusion.11 = f16[16,8,4,1024]{3,0,2,1:T(8,128)(2,1)S(1)} fusion(f32[8,16,4,1024]{3,1,2,0:T(8,128)} %get-tuple-element.32, f32[]{:T(128)S(6)} %exp2.15), kind=kLoop, calls=%fused_computation.21 | loop fusion | flops 1048576 | bytes 3145732 | tf_op jit(solution)/shard_map/convert_element_type | solution.py:37
  13.6 1.6 %copy.45 = f16[16,8,4,1024]{3,1,2,0:T(8,128)(2,1)} copy(f16[16,8,4,1024]{3,0,2,1:T(8,128)(2,1)S(1)} %fusion.11) | data formatting | bytes 2097152 | tf_op jit(solution)/shard_map/reshape | solution.py:38
  15.4 2.6 %pad_maximum_fusion = f16[8,2,8,4,1152]{4,2,3,1,0:T(8,128)(2,1)} fusion(f16[8,2,8,4,128]{4,2,3,1,0:T(8,128)(2,1)S(1)} %broadcast_in_dim.64, f16[8,2,8,4,1024]{4,2,3,1,0:T(8,128)(2,1)} %bitcast.76), kind=kLoop, calls=%fused_computation.19 | loop fusion | flops 589824 | bytes 2359296 | tf_op jit(solution)/shard_map/concatenate | solution.py:48
  17.9 9.0 %all-to-all-start = ((f16[8,2,8,4,1152]{4,2,3,1,0:T(8,128)(2,1)}), f16[8,2,8,4,1152]{4,2,3,1,0:T(8,128)(2,1)}, u32[]{:S(2)}, u32[]{:S(2)}) async-start(f16[8,2,8,4,1152]{4,2,3,1,0:T(8,128)(2,1)} %pad_maximum_fusion), calls=%async_computation | async-start | bytes 2359296 | tf_op jit(solution)/shard_map/all_to_all | solution.py:59
  27.0 28.3 %all_gather.4 = f32[32,2,32,64]{3,2,1,0:T(8,128)} all-gather(f32[1,2,32,64]{3,2,1,0:T(8,128)S(1)} %dynamic_update_slice.5), channel_id=1, replica_groups=mesh['pair'=32,'lam'=8] {'pair'}, dimensions={0}, use_global_device_ids=true | all-gather | bytes 540672 | tf_op jit(solution)/shard_map/all_gather | solution.py:8
  55.5 1.3 %reduce_sum.9 = f32[2,32,64]{2,1,0:T(8,128)S(1)} reduce(f32[32,2,32,64]{3,2,1,0:T(8,128)} %all_gather.4, f32[]{:T(128)} %constant.125.clone.1), dimensions={0}, to_apply=%region_3.4 | reduce | flops 126976 | bytes 540676 | tf_op jit(solution)/shard_map/reduce_sum | solution.py:9
  57.1 6.2 %gather_fusion.1 = bf16[2048,16]{1,0:T(8,128)(2,1)S(1)} fusion(bf16[1024,16]{1,0:T(8,128)(2,1)S(1)} %copy.39, s32[2048]{0:T(1024)S(1)} %broadcast_clamp_fusion.1), kind=kCustom, calls=%fused_computation.1 | custom fusion | bytes 139264 | tf_op jit(solution)/shard_map/jit(_take)/gather | solution.py:76
  63.5 0.7 fusion.20
  64.5 2.2 %fusion.10 = bf16[2,16,4,1024]{3,1,2,0:T(8,128)(2,1)S(1)} fusion(f16[8,2,8,4,1152]{4,2,3,1,0:T(8,128)(2,1)} %all-to-all-done, f32[8,8,128]{2,1,0:T(8,128)S(1)} %fusion.20, f32[8]{0:T(128)S(1)} %fusion.26), kind=kOutput, calls=%fused_computation.20 | convolution fusion | flops 100795392 | bytes 1343520 | tf_op jit(solution)/shard_map/ptg,pjtks->jgks/dot_general | solution.py:63
  67.5 0.9 copy.37
  68.4 1.3 %reshape.244 = bf16[2,64,32,40]{1,0,3,2:T(2,128)(2,1)S(1)} reshape(bf16[128,1280]{0,1:T(8,128)(2,1)} %copy.37) | data formatting | bytes 655360 | tf_op jit(solution)/shard_map/reshape | solution.py:72
  69.7 1.1 %reshape.278 = bf16[32,2,2560]{2,1,0:T(2,128)(2,1)} reshape(bf16[32,40,2,64]{3,2,1,0:T(2,128)(2,1)S(1)} %bitcast.77) | data formatting | bytes 655360
  70.8 5.2 %all-to-all-start.1 = ((bf16[32,2,2560]{2,1,0:T(2,128)(2,1)}), bf16[32,2,2560]{2,1,0:T(2,128)(2,1)}, u32[]{:S(2)}, u32[]{:S(2)}) async-start(bf16[32,2,2560]{2,1,0:T(2,128)(2,1)} %reshape.278), calls=%async_computation.1 | async-start | bytes 655360 | tf_op jit(solution)/shard_map/all_to_all | solution.py:73
  76.1 9.8 %gather_fusion.2 = bf16[2048,1280]{1,0:T(8,128)(2,1)} fusion(bf16[1024,1280]{1,0:T(8,128)(2,1)S(1)} %copy-done, s32[2048]{0:T(1024)S(1)} %broadcast_clamp_fusion), kind=kCustom, calls=%fused_computation.2 | custom fusion | bytes 10493952 | tf_op jit(solution)/shard_map/jit(_take)/gather | solution.py:77
  86.0 1.4 %reshape.279 = bf16[32,40,2,64]{3,2,1,0:T(2,128)(2,1)S(1)} reshape(bf16[32,2,2560]{2,1,0:T(2,128)(2,1)} %all-to-all-done.1) | data formatting | bytes 655360
  87.9 1.5 %copy.38 = f32[2,32,64,1,40]{2,1,4,0,3:T(8,128)} copy(f32[2,32,64,1,40]{2,0,4,1,3:T(2,128)S(1)} %convert_bitcast_fusion) | data formatting | bytes 1310720 | tf_op jit(solution)/shard_map/convert_element_type | solution.py:79
  89.3 1.7 %reshape.247 = f32[2,2048,40]{1,2,0:T(8,128)S(1)} reshape(f32[2,32,64,1,40]{2,1,4,0,3:T(8,128)} %copy.38) | data formatting | bytes 1310720 | tf_op jit(solution)/shard_map/convert_element_type | solution.py:79
  91.1 11.6 %fusion = f32[2,40,16,1280]{3,2,1,0:T(8,128)} fusion(bf16[2048,1280]{1,0:T(8,128)(2,1)} %gather_fusion.2, f32[2048,16]{0,1:T(8,128)S(1)} %select_convert_fusion, f32[2,2048,40]{1,2,0:T(8,128)S(1)} %reshape.247, pred[2048]{0:T(1024)(128)(4,1)S(1)} %compare_and_fusion), kind=kOutput, calls=%fused_computation.4 | convolution fusion | flops 6718750720 | bytes 12584960 | tf_op jit(solution)/shard_map/qrbi,ra->qbia/dot_general | solution.py:82
  102.6 7.7 %reshape.245 = f32[2,40,20480]{2,1,0:T(8,128)} reshape(f32[2,40,16,1280]{3,2,1,0:T(8,128)} %fusion) | data formatting | bytes 13107200 | tf_op jit(solution)/shard_map/reshape | solution.py:83
  (45 shorter events, 4.3 us)
Async XLA Ops:
  0.0 67.0 %copy-start = (bf16[1024,1280]{1,0:T(8,128)(2,1)S(1)}, bf16[1024,1280]{1,0:T(8,128)(2,1)}, u32[]{:S(2)}) copy-start(bf16[1024,1280]{1,0:T(8,128)(2,1)} %param.19) | copy-start | bytes 7864324
  4.8 5.6 %copy-start.4 = (s32[1,8]{1,0:T(1,128)S(1)}, s32[1,8]{1,0:T(1,128)}, u32[]{:S(2)}) copy-start(s32[1,8]{1,0:T(1,128)} %param.13) | copy-start | bytes 100
  15.2 11.7 %copy-start.2 = (s32[64]{0:T(128)S(1)}, s32[64]{0:T(128)}, u32[]{:S(2)}) copy-start(s32[64]{0:T(128)} %param.17) | copy-start | bytes 772
  15.2 11.7 %copy-start.3 = (s32[64]{0:T(128)S(1)}, s32[64]{0:T(128)}, u32[]{:S(2)}) copy-start(s32[64]{0:T(128)} %param.16) | copy-start | bytes 772
  15.4 40.0 %copy-start.1 = (bf16[1024,16]{0,1:T(8,128)(2,1)S(1)}, bf16[1024,16]{0,1:T(8,128)(2,1)}, u32[]{:S(2)}) copy-start(bf16[1024,16]{0,1:T(8,128)(2,1)} %param.18) | copy-start | bytes 98308
  17.9 45.6 %all-to-all-start = ((f16[8,2,8,4,1152]{4,2,3,1,0:T(8,128)(2,1)}), f16[8,2,8,4,1152]{4,2,3,1,0:T(8,128)(2,1)}, u32[]{:S(2)}, u32[]{:S(2)}) async-start(f16[8,2,8,4,1152]{4,2,3,1,0:T(8,128)(2,1)} %pad_maximum_fusion), calls=%async_computation | async-start | bytes 2359296 | tf_op jit(solution)/shard_map/all_to_all | solution.py:59
  70.8 15.2 %all-to-all-start.1 = ((bf16[32,2,2560]{2,1,0:T(2,128)(2,1)}), bf16[32,2,2560]{2,1,0:T(2,128)(2,1)}, u32[]{:S(2)}, u32[]{:S(2)}) async-start(bf16[32,2,2560]{2,1,0:T(2,128)(2,1)} %reshape.278), calls=%async_computation.1 | async-start | bytes 655360 | tf_op jit(solution)/shard_map/all_to_all | solution.py:73
